TPU v7x, 128 devices: a whole 4x4x4 slice. The times are simulated.
128 devices in a mesh: row: 64 (over y, x, z_lo, core), col: 2 (over z_hi).
Axes of the slice: x: 4, y: 4, z: 4 (z_hi: 2, z_lo: 2; z = z_hi * 2 + z_lo), core: 2. Of those that a mesh axis runs over, the one named last changes fastest.
Arguments:
- dist_first: bfloat16 [32768, 32768], P('row', 'col'), may hold values from -0.34 to 0.34
- coupling: bfloat16 [32768, 256], P('row', 'col'), may hold values from 0.099609375 to 1
- dist_second: bfloat16 [256, 512], P(None, 'col'), may hold values from -12 to 12
- row_potential: float32 [32768], P('row'), may hold values from -150 to 120
- column_cost: float32 [512], P('col'), may hold values from -300 to 20
- column_mass: float32 [512], P('col'), may hold values from 0.5 to 2
Outputs:
- transport: bfloat16 [32768, 512], P('row', 'col')
- potential: float32 [512], P('col')
All inputs are finite; a program needn't handle non-finite values.
Results may differ from a plain program's by a relative error of at most 0.0051.
Values may be sent and summed in bfloat16 or wider, within the bound.
No kernel may reach another device: no remote copies, remote signals or barrier semaphores. Data moves between devices by JAX's collectives and lax.ppermute only.
A program may use at most 128 MiB of HBM per device.

v0:
```python
import jax
import jax.numpy as jnp
import numpy as np
from jax import lax
from jax.sharding import Mesh
from jax.sharding import PartitionSpec as P

N = 32768
AXES = ("yh", "yl", "x", "zl", "core", "zh")
ROWS = ("yh", "yl", "x", "zl", "core")
GATHER = ("yl", "x", "zl", "core")


def body(dist_first, coupling, dist_second, row_potential, column_cost, column_mass):
    zh = lax.axis_index("zh")
    yh = lax.axis_index("yh")
    blocks = coupling.shape[0]
    k_half = coupling.shape[1]
    q_half = dist_second.shape[1]
    coupling_x = lax.ppermute(coupling, "zh", [(0, 1), (1, 0)])
    second_x = lax.ppermute(dist_second, "zh", [(0, 1), (1, 0)])
    piece = jnp.concatenate([coupling, coupling_x], axis=1)
    into_other_half = [(0, 4), (2, 6), (5, 1), (7, 3)]
    moved = lax.ppermute(piece, ("yh", "yl", "zh"), into_other_half)
    piece = jnp.where(yh == zh, piece, moved)
    gathered = lax.all_gather(piece, GATHER, axis=0, tiled=True)
    second_full = jnp.concatenate([dist_second, second_x], axis=1)
    second_k = jnp.concatenate(
        [
            lax.dynamic_slice_in_dim(second_full, zh * k_half, k_half, axis=0),
            lax.dynamic_slice_in_dim(second_full, (1 - zh) * k_half, k_half, axis=0),
        ]
    )

    def partial_gradient(cols):
        product = jnp.dot(gathered, second_k[:, cols], preferred_element_type=jnp.float32).astype(
            jnp.bfloat16
        )
        return jnp.dot(dist_first, product, preferred_element_type=jnp.float32)

    other_part = partial_gradient(slice(q_half, 2 * q_half))
    arrived = lax.ppermute(other_part, "zh", [(0, 1), (1, 0)])
    own_part = partial_gradient(slice(0, q_half))
    own_part, arrived = lax.optimization_barrier((own_part, arrived))
    gradient = own_part + arrived
    scores = row_potential[:, None] + 2.0 * gradient - column_cost[None, :]
    local_high = jnp.max(scores, axis=0)
    local_sum = jnp.sum(jnp.exp(scores - local_high[None, :]), axis=0)
    stats = lax.all_gather(jnp.stack([local_high, local_sum]), ROWS, axis=0, tiled=False)
    highest = jnp.max(stats[:, 0], axis=0)
    column_sum = jnp.sum(stats[:, 1] * jnp.exp(stats[:, 0] - highest[None, :]), axis=0)
    weights = jnp.exp(scores - highest[None, :])
    potential = jnp.log(column_mass) - highest - jnp.log(column_sum)
    transport = (weights * (N * column_mass / column_sum)[None, :]).astype(jnp.bfloat16)
    return (transport, potential)


def solution(mesh):
    devices = np.asarray(mesh.devices).reshape(2, 2, 4, 2, 2, 2)
    fine = Mesh(devices, AXES)
    in_specs = (P(ROWS, "zh"), P(ROWS, "zh"), P(None, "zh"), P(ROWS), P("zh"), P("zh"))
    out_specs = (P(ROWS, "zh"), P("zh"))
    return jax.shard_map(body, mesh=fine, in_specs=in_specs, out_specs=out_specs, check_vma=False)
```

profile of v0, /device:TPU:1, one launch (start us, length us, event | category | flops | bytes accessed | tf_op | source)
XLA Modules:
  0.0 210.5 jit_solution(4188174330190762667)
XLA Ops:
  7.2 0.0 all-gather.4.cloned.1.call-start
  7.2 4.5 %collective-permute-start = (bf16[512,128]{1,0:T(8,128)(2,1)}, bf16[512,128]{1,0:T(8,128)(2,1)S(1)}, u32[]{:S(2)}, u32[]{:S(2)}) collective-permute-start(bf16[512,128]{1,0:T(8,128)(2,1)} %param.7), channel_id=1, source_target_pairs={{0,1},{1,0},{2,3},{3,2},{4,5},{5,4},{6,7},{7,6},{8,9},{9,8},{10,11... | collective-permute-start | bytes 393224 | tf_op jit(solution)/shard_map/ppermute | solution.py:20
  11.7 1.0 constant_dynamic-update-slice_fusion.1
  12.7 2.5 %collective-permute-done = bf16[512,128]{1,0:T(8,128)(2,1)S(1)} collective-permute-done((bf16[512,128]{1,0:T(8,128)(2,1)}, bf16[512,128]{1,0:T(8,128)(2,1)S(1)}, u32[]{:S(2)}, u32[]{:S(2)}) %collective-permute-start) | collective-permute-done | bytes 131104 | tf_op jit(solution)/shard_map/ppermute | solution.py:20
  15.2 4.8 %collective-permute-start.1 = (bf16[512,256]{1,0:T(8,128)(2,1)S(1)}, bf16[512,256]{1,0:T(8,128)(2,1)S(1)}, u32[]{:S(2)}, u32[]{:S(2)}) collective-permute-start(bf16[512,256]{1,0:T(8,128)(2,1)S(1)} %constant_dynamic-update-slice_fusion), channel_id=1, source_target_pairs={{0,64},{32,96},{65,1},{97,33},{2,66},{34,98},{67,3},{99,35},{4,68}... | collective-permute-start | bytes 786440 | tf_op jit(solution)/shard_map/ppermute | solution.py:24
  20.0 4.3 %collective-permute-done.1 = bf16[512,256]{1,0:T(8,128)(2,1)S(1)} collective-permute-done((bf16[512,256]{1,0:T(8,128)(2,1)S(1)}, bf16[512,256]{1,0:T(8,128)(2,1)S(1)}, u32[]{:S(2)}, u32[]{:S(2)}) %collective-permute-start.1) | collective-permute-done | bytes 262176 | tf_op jit(solution)/shard_map/ppermute | solution.py:24
  24.4 0.7 broadcast_select_fusion
  25.1 0.0 all-gather.4.cloned.1.call-update
  25.1 3.2 %collective-permute-start.2 = (bf16[256,256]{1,0:T(8,128)(2,1)}, bf16[256,256]{1,0:T(8,128)(2,1)S(1)}, u32[]{:S(2)}, u32[]{:S(2)}) collective-permute-start(bf16[256,256]{1,0:T(8,128)(2,1)} %param.8), channel_id=1, source_target_pairs={{0,1},{1,0},{2,3},{3,2},{4,5},{5,4},{6,7},{7,6},{8,9},{9,8},{10,11... | collective-permute-start | bytes 393224 | tf_op jit(solution)/shard_map/ppermute | solution.py:21
  28.3 0.9 constant_dynamic-update-slice_fusion.3
  29.3 1.6 collective-permute-done.2
  30.9 63.0 %all-gather.4.cloned.1.call-done = bf16[16384,256]{1,0:T(8,128)(2,1)} async-done(((bf16[512,256]{1,0:T(8,128)(2,1)}), bf16[16384,256]{1,0:T(8,128)(2,1)}) %all-gather.4.cloned.1.call-update) | async-done | bytes 8388624 | tf_op jit(solution)/shard_map/all_gather | solution.py:26
  93.9 11.7 %fusion.2 = f32[512,256]{0,1:T(8,128)S(1)} fusion(bf16[512,16384]{1,0:T(8,128)(2,1)} %param.6, bf16[16384,256]{1,0:T(8,128)(2,1)} %all-gather.4.cloned.1.call-done, bf16[128,512]{1,0:T(8,128)(2,1)S(1)} %get-tuple-element.12, bf16[128,512]{1,0:T(8,128)(2,1)S(1)} %get-tuple-element.13), kind=kOutput, calls=%fused_computation.4 | convolution fusion | flops 6446907392 | bytes 25952256 | tf_op jit(solution)/shard_map/dot_general | solution.py:39
  105.6 0.0 copy-start
  105.6 0.0 copy-start.1
  105.7 0.0 copy-start.2
  105.7 2.5 %collective-permute-start.3 = (f32[512,256]{0,1:T(8,128)S(1)}, f32[512,256]{0,1:T(8,128)S(1)}, u32[]{:S(2)}, u32[]{:S(2)}) collective-permute-start(f32[512,256]{0,1:T(8,128)S(1)} %fusion.2), channel_id=1, source_target_pairs={{0,1},{1,0},{2,3},{3,2},{4,5},{5,4},{6,7},{7,6},{8,9},{9,8},{10,11... | collective-permute-start | bytes 1572872 | tf_op jit(solution)/shard_map/ppermute | solution.py:42
  108.2 11.7 %fusion.3 = f32[512,256]{0,1:T(8,128)S(1)} fusion(bf16[512,16384]{1,0:T(8,128)(2,1)} %param.6, bf16[16384,256]{1,0:T(8,128)(2,1)} %all-gather.4.cloned.1.call-done, bf16[128,512]{1,0:T(8,128)(2,1)S(1)} %get-tuple-element.13, bf16[128,512]{1,0:T(8,128)(2,1)S(1)} %get-tuple-element.12), kind=kOutput, calls=%fused_computation.5 | convolution fusion | flops 6446907392 | bytes 25952256 | tf_op jit(solution)/shard_map/dot_general | solution.py:39
  119.9 0.6 collective-permute-done.3
  120.5 0.0 copy-done
  120.5 0.0 copy-done.1
  120.5 0.2 fusion.16
  120.7 0.2 exponential_reduce_fusion
  120.9 80.9 %all-gather.1 = f32[64,2,256]{2,1,0:T(2,128)S(1)} all-gather(f32[1,2,256]{2,1,0:T(2,128)S(1)} %maximum_bitcast_fusion), channel_id=2, replica_groups=mesh['yh'=2,'yl'=2,'x'=4,'zl'=2,'core'=2,'zh'=2] {'yh','yl','x','zl','co..., dimensions={0}, use_global_device_ids=true | all-gather | bytes 133120 | tf_op jit(solution)/shard_map/all_gather | solution.py:49
  201.9 0.1 slice_reduce_fusion
  202.1 0.0 copy-done.2
  202.1 0.6 log_subtract_fusion
  202.6 0.1 multiply_convert_fusion
  202.8 0.8 copy.11
  (5 shorter events, 0.1 us)
Async XLA Ops:
  7.2 86.8 %all-gather.4.cloned.1.call-start = ((), (), s32[]{:S(2)}) async-start(), calls=%async_computation | async-start | bytes 8650752 | tf_op jit(solution)/shard_map/all_gather | solution.py:26
  7.2 7.9 %collective-permute-start = (bf16[512,128]{1,0:T(8,128)(2,1)}, bf16[512,128]{1,0:T(8,128)(2,1)S(1)}, u32[]{:S(2)}, u32[]{:S(2)}) collective-permute-start(bf16[512,128]{1,0:T(8,128)(2,1)} %param.7), channel_id=1, source_target_pairs={{0,1},{1,0},{2,3},{3,2},{4,5},{5,4},{6,7},{7,6},{8,9},{9,8},{10,11... | collective-permute-start | bytes 393224 | tf_op jit(solution)/shard_map/ppermute | solution.py:20
  15.2 9.2 %collective-permute-start.1 = (bf16[512,256]{1,0:T(8,128)(2,1)S(1)}, bf16[512,256]{1,0:T(8,128)(2,1)S(1)}, u32[]{:S(2)}, u32[]{:S(2)}) collective-permute-start(bf16[512,256]{1,0:T(8,128)(2,1)S(1)} %constant_dynamic-update-slice_fusion), channel_id=1, source_target_pairs={{0,64},{32,96},{65,1},{97,33},{2,66},{34,98},{67,3},{99,35},{4,68}... | collective-permute-start | bytes 786440 | tf_op jit(solution)/shard_map/ppermute | solution.py:24
  25.1 5.8 %collective-permute-start.2 = (bf16[256,256]{1,0:T(8,128)(2,1)}, bf16[256,256]{1,0:T(8,128)(2,1)S(1)}, u32[]{:S(2)}, u32[]{:S(2)}) collective-permute-start(bf16[256,256]{1,0:T(8,128)(2,1)} %param.8), channel_id=1, source_target_pairs={{0,1},{1,0},{2,3},{3,2},{4,5},{5,4},{6,7},{7,6},{8,9},{9,8},{10,11... | collective-permute-start | bytes 393224 | tf_op jit(solution)/shard_map/ppermute | solution.py:21
  105.6 14.9 %copy-start = (f32[512]{0:T(512)S(1)}, f32[512]{0:T(512)}, u32[]{:S(2)}) copy-start(f32[512]{0:T(512)} %param.9) | copy-start | bytes 6148
  105.6 14.9 %copy-start.1 = (f32[256]{0:T(256)S(1)}, f32[256]{0:T(256)}, u32[]{:S(2)}) copy-start(f32[256]{0:T(256)} %param.10) | copy-start | bytes 3076
  105.7 96.4 %copy-start.2 = (f32[256]{0:T(256)S(1)}, f32[256]{0:T(256)}, u32[]{:S(2)}) copy-start(f32[256]{0:T(256)} %param.11) | copy-start | bytes 3076
  105.7 14.8 %collective-permute-start.3 = (f32[512,256]{0,1:T(8,128)S(1)}, f32[512,256]{0,1:T(8,128)S(1)}, u32[]{:S(2)}, u32[]{:S(2)}) collective-permute-start(f32[512,256]{0,1:T(8,128)S(1)} %fusion.2), channel_id=1, source_target_pairs={{0,1},{1,0},{2,3},{3,2},{4,5},{5,4},{6,7},{7,6},{8,9},{9,8},{10,11... | collective-permute-start | bytes 1572872 | tf_op jit(solution)/shard_map/ppermute | solution.py:42
Sparse Core Ops, SparseCore 0:
  25.2 68.6 all-gather.3
where the time goes:
time: 211 us; the launch traced here: 210 us
  blocking collectives  80.9 us (38%)
  waiting for transfers between devices  72.1 us (34%)
  matrix products  23.4 us (11%)
  starting transfers between devices  15.1 us (7%)
  between operations  14.1 us (7%)
  local copies, waits for them, and re-layouts  2.84 us (1%)
    all_gather x1, blocking collectives, body(): lax.all_gather(jnp.stack([local_high, local_sum]), ROWS, axis=0, tiled=Fa...  80.9 us
    all_gather x1, waiting for transfers between devices, body(): gathered = lax.all_gather(piece, GATHER, axis=0, tiled=True)  63 us
    dot_general x2, matrix products, partial_gradient(): return jnp.dot(dist_first, product, preferred_element_type=jnp.float32)  23.4 us
    ppermute x1, starting transfers between devices, body(): moved = lax.ppermute(piece, ('yh', 'yl', 'zh'), into_other_half)  4.83 us
    ppermute x1, starting transfers between devices, body(): coupling_x = lax.ppermute(coupling, 'zh', [(0, 1), (1, 0)])  4.51 us
    ppermute x1, waiting for transfers between devices, body(): moved = lax.ppermute(piece, ('yh', 'yl', 'zh'), into_other_half)  4.33 us
  transfers between devices with their start and end apart: 5, of which 5 were waited for; matrix products, arithmetic and copies ran while one was open for 6% of the time, Pallas kernels for 0%

commit v1 on v0

--- a/solution.py
+++ b/solution.py
@@ -23,7 +23,9 @@
     into_other_half = [(0, 4), (2, 6), (5, 1), (7, 3)]
     moved = lax.ppermute(piece, ("yh", "yl", "zh"), into_other_half)
     piece = jnp.where(yh == zh, piece, moved)
-    gathered = lax.all_gather(piece, GATHER, axis=0, tiled=True)
+    gathered = jnp.concatenate(
+        lax.all_to_all(jnp.stack([piece] * lax.axis_size(GATHER)), GATHER, 0, 0), axis=0
+    )
     second_full = jnp.concatenate([dist_second, second_x], axis=1)
     second_k = jnp.concatenate(
         [

time: 211 us -> 251 us (1.19)
  waiting for transfers between devices: 72.1 us -> 107 us
  between operations: 14.1 us -> 0.77 us
  starting transfers between devices: 15.1 us -> 26.8 us
  blocking collectives: 80.9 us -> 85.2 us
  local copies, waits for them, and re-layouts: 2.84 us -> 6.08 us
    all_gather x1 -> x0, waiting for transfers between devices: 63 us -> none  [body(): gathered = lax.all_gather(piece, GATHER, axis=0, tiled=True)]
    ppermute x1, waiting for transfers between devices: 1.62 us -> 60.1 us  [body(): second_x = lax.ppermute(dist_second, 'zh', [(0, 1), (1, 0)])]
    all_to_all x0 -> x1, waiting for transfers between devices: none -> 39.8 us  [body(): lax.all_to_all(jnp.stack([piece] * lax.axis_size(GATHER)), GATHER, 0, 0)]
    all_to_all x0 -> x1, starting transfers between devices: none -> 7.31 us  [body(): lax.all_to_all(jnp.stack([piece] * lax.axis_size(GATHER)), GATHER, 0, 0)]
    all_gather x1, blocking collectives: 80.9 us -> 85.2 us  [body(): lax.all_gather(jnp.stack([local_high, local_sum]), ROWS, axis=0, tiled=Fa...]
    another operation x0 -> x1, local copies, waits for them, and re-layouts: none -> 4.17 us  [body(): jnp.stack([piece] * lax.axis_size(GATHER))]
    ppermute x1, starting transfers between devices: 2.49 us -> 5.08 us  [body(): arrived = lax.ppermute(other_part, 'zh', [(0, 1), (1, 0)])]
  transfers between devices with their start and end apart: 5 -> 5, of which waited for: 5 -> 4; matrix products, arithmetic and copies ran while one was open for 6% -> 5% of each run, Pallas kernels for 0% -> 0%
where the time goes in v1:
time: 251 us; the launch traced here: 250 us
  waiting for transfers between devices  107 us (43%)
  blocking collectives  85.2 us (34%)
  starting transfers between devices  26.8 us (11%)
  matrix products  23.4 us (9%)
  local copies, waits for them, and re-layouts  6.08 us (2%)
    all_gather x1, blocking collectives, body(): lax.all_gather(jnp.stack([local_high, local_sum]), ROWS, axis=0, tiled=Fa...  85.2 us
    ppermute x1, waiting for transfers between devices, body(): second_x = lax.ppermute(dist_second, 'zh', [(0, 1), (1, 0)])  60.1 us
    all_to_all x1, waiting for transfers between devices, body(): lax.all_to_all(jnp.stack([piece] * lax.axis_size(GATHER)), GATHER, 0, 0)  39.8 us
    dot_general x2, matrix products, partial_gradient(): return jnp.dot(dist_first, product, preferred_element_type=jnp.float32)  23.4 us
    all_to_all x1, starting transfers between devices, body(): lax.all_to_all(jnp.stack([piece] * lax.axis_size(GATHER)), GATHER, 0, 0)  7.31 us
    ppermute x1, starting transfers between devices, body(): arrived = lax.ppermute(other_part, 'zh', [(0, 1), (1, 0)])  5.08 us
    ppermute x1, starting transfers between devices, body(): second_x = lax.ppermute(dist_second, 'zh', [(0, 1), (1, 0)])  5.07 us
  transfers between devices with their start and end apart: 5, of which 4 were waited for; matrix products, arithmetic and copies ran while one was open for 5% of the time, Pallas kernels for 0%

profile of v1, /device:TPU:1, one launch (start us, length us, event | category | flops | bytes accessed | tf_op | source)
XLA Modules:
  0.0 250.4 jit_solution(10975865531687640288)
XLA Ops:
  0.6 4.5 %collective-permute-start = (bf16[512,128]{1,0:T(8,128)(2,1)}, bf16[512,128]{1,0:T(8,128)(2,1)S(1)}, u32[]{:S(2)}, u32[]{:S(2)}) collective-permute-start(bf16[512,128]{1,0:T(8,128)(2,1)} %param.7), channel_id=1, source_target_pairs={{0,1},{1,0},{2,3},{3,2},{4,5},{5,4},{6,7},{7,6},{8,9},{9,8},{10,11... | collective-permute-start | bytes 393224 | tf_op jit(solution)/shard_map/ppermute | solution.py:20
  5.1 1.0 constant_dynamic-update-slice_fusion.1
  6.1 2.5 collective-permute-done
  8.6 4.8 %collective-permute-start.1 = (bf16[512,256]{1,0:T(8,128)(2,1)S(1)}, bf16[512,256]{1,0:T(8,128)(2,1)S(1)}, u32[]{:S(2)}, u32[]{:S(2)}) collective-permute-start(bf16[512,256]{1,0:T(8,128)(2,1)S(1)} %constant_dynamic-update-slice_fusion), channel_id=1, source_target_pairs={{0,64},{32,96},{65,1},{97,33},{2,66},{34,98},{67,3},{99,35},{4,68}... | collective-permute-start | bytes 786440 | tf_op jit(solution)/shard_map/ppermute | solution.py:24
  13.5 4.3 %collective-permute-done.1 = bf16[512,256]{1,0:T(8,128)(2,1)S(1)} collective-permute-done((bf16[512,256]{1,0:T(8,128)(2,1)S(1)}, bf16[512,256]{1,0:T(8,128)(2,1)S(1)}, u32[]{:S(2)}, u32[]{:S(2)}) %collective-permute-start.1) | collective-permute-done | bytes 262176 | tf_op jit(solution)/shard_map/ppermute | solution.py:24
  17.8 4.2 %stack.8 = bf16[32,512,256]{2,1,0:T(8,128)(2,1)} broadcast(bf16[512,256]{1,0:T(8,128)(2,1)S(1)} %broadcast_select_fusion), dimensions={1,2} | broadcast | bytes 8650752 | tf_op jit(solution)/shard_map/stack | solution.py:27
  22.0 0.0 copy-start
  22.0 7.3 %all-to-all-start = ((bf16[32,512,256]{2,1,0:T(8,128)(2,1)}), bf16[32,512,256]{2,1,0:T(8,128)(2,1)}, u32[]{:S(2)}, u32[]{:S(2)}) async-start(bf16[32,512,256]{2,1,0:T(8,128)(2,1)} %stack.8), calls=%async_computation | async-start | bytes 16777216 | tf_op jit(solution)/shard_map/all_to_all | solution.py:27
  29.3 0.0 copy-done
  29.3 5.1 %collective-permute-start.2 = (bf16[256,256]{1,0:T(8,128)(2,1)S(1)}, bf16[256,256]{1,0:T(8,128)(2,1)S(1)}, u32[]{:S(2)}, u32[]{:S(2)}) collective-permute-start(bf16[256,256]{1,0:T(8,128)(2,1)S(1)} %copy-done), channel_id=1, source_target_pairs={{0,1},{1,0},{2,3},{3,2},{4,5},{5,4},{6,7},{7,6},{8,9},{9,8},{10,11... | collective-permute-start | bytes 393224 | tf_op jit(solution)/shard_map/ppermute | solution.py:21
  34.4 60.1 %collective-permute-done.2 = bf16[256,256]{1,0:T(8,128)(2,1)S(1)} collective-permute-done((bf16[256,256]{1,0:T(8,128)(2,1)S(1)}, bf16[256,256]{1,0:T(8,128)(2,1)S(1)}, u32[]{:S(2)}, u32[]{:S(2)}) %collective-permute-start.2) | collective-permute-done | bytes 131104 | tf_op jit(solution)/shard_map/ppermute | solution.py:21
  94.6 39.8 %all-to-all-done = bf16[32,512,256]{2,1,0:T(8,128)(2,1)} async-done(((bf16[32,512,256]{2,1,0:T(8,128)(2,1)}), bf16[32,512,256]{2,1,0:T(8,128)(2,1)}, u32[]{:S(2)}, u32[]{:S(2)}) %all-to-all-start) | async-done | bytes 8388640 | tf_op jit(solution)/shard_map/all_to_all | solution.py:27
  134.4 11.7 %fusion.2 = f32[512,256]{0,1:T(8,128)S(1)} fusion(bf16[512,16384]{1,0:T(8,128)(2,1)} %param.6, bf16[16384,256]{1,0:T(8,128)(2,1)} %bitcast, bf16[128,512]{1,0:T(8,128)(2,1)S(1)} %get-tuple-element.12, bf16[128,512]{1,0:T(8,128)(2,1)S(1)} %get-tuple-element.13), kind=kOutput, calls=%fused_computation.4 | convolution fusion | flops 6446907392 | bytes 25952256 | tf_op jit(solution)/shard_map/dot_general | solution.py:41
  146.1 0.0 copy-start.1
  146.1 0.0 copy-start.2
  146.1 0.0 copy-start.3
  146.1 5.1 %collective-permute-start.3 = (f32[512,256]{0,1:T(8,128)S(1)}, f32[512,256]{0,1:T(8,128)S(1)}, u32[]{:S(2)}, u32[]{:S(2)}) collective-permute-start(f32[512,256]{0,1:T(8,128)S(1)} %fusion.2), channel_id=1, source_target_pairs={{0,1},{1,0},{2,3},{3,2},{4,5},{5,4},{6,7},{7,6},{8,9},{9,8},{10,11... | collective-permute-start | bytes 1572872 | tf_op jit(solution)/shard_map/ppermute | solution.py:44
  151.2 11.7 %fusion.3 = f32[512,256]{0,1:T(8,128)S(1)} fusion(bf16[512,16384]{1,0:T(8,128)(2,1)} %param.6, bf16[16384,256]{1,0:T(8,128)(2,1)} %bitcast, bf16[128,512]{1,0:T(8,128)(2,1)S(1)} %get-tuple-element.13, bf16[128,512]{1,0:T(8,128)(2,1)S(1)} %get-tuple-element.12), kind=kOutput, calls=%fused_computation.5 | convolution fusion | flops 6446907392 | bytes 25952256 | tf_op jit(solution)/shard_map/dot_general | solution.py:41
  162.9 0.0 collective-permute-done.3
  162.9 0.0 copy-done.1
  162.9 0.0 copy-done.2
  163.0 0.2 fusion.16
  163.2 0.2 exponential_reduce_fusion
  163.4 85.2 %all-gather.1 = f32[64,2,256]{2,1,0:T(2,128)S(1)} all-gather(f32[1,2,256]{2,1,0:T(2,128)S(1)} %maximum_bitcast_fusion), channel_id=2, replica_groups=mesh['yh'=2,'yl'=2,'x'=4,'zl'=2,'core'=2,'zh'=2] {'yh','yl','x','zl','co..., dimensions={0}, use_global_device_ids=true | all-gather | bytes 133120 | tf_op jit(solution)/shard_map/all_gather | solution.py:51
  248.6 0.1 slice_reduce_fusion
  248.8 0.0 copy-done.3
  248.8 0.6 log_subtract_fusion
  249.4 0.1 multiply_convert_fusion
  249.6 0.8 copy.11
  (7 shorter events, 0.2 us)
Async XLA Ops:
  0.6 7.9 %collective-permute-start = (bf16[512,128]{1,0:T(8,128)(2,1)}, bf16[512,128]{1,0:T(8,128)(2,1)S(1)}, u32[]{:S(2)}, u32[]{:S(2)}) collective-permute-start(bf16[512,128]{1,0:T(8,128)(2,1)} %param.7), channel_id=1, source_target_pairs={{0,1},{1,0},{2,3},{3,2},{4,5},{5,4},{6,7},{7,6},{8,9},{9,8},{10,11... | collective-permute-start | bytes 393224 | tf_op jit(solution)/shard_map/ppermute | solution.py:20
  8.6 9.2 %collective-permute-start.1 = (bf16[512,256]{1,0:T(8,128)(2,1)S(1)}, bf16[512,256]{1,0:T(8,128)(2,1)S(1)}, u32[]{:S(2)}, u32[]{:S(2)}) collective-permute-start(bf16[512,256]{1,0:T(8,128)(2,1)S(1)} %constant_dynamic-update-slice_fusion), channel_id=1, source_target_pairs={{0,64},{32,96},{65,1},{97,33},{2,66},{34,98},{67,3},{99,35},{4,68}... | collective-permute-start | bytes 786440 | tf_op jit(solution)/shard_map/ppermute | solution.py:24
  22.0 7.3 %copy-start = (bf16[256,256]{1,0:T(8,128)(2,1)S(1)}, bf16[256,256]{1,0:T(8,128)(2,1)}, u32[]{:S(2)}) copy-start(bf16[256,256]{1,0:T(8,128)(2,1)} %param.8) | copy-start | bytes 393220
  22.0 112.4 %all-to-all-start = ((bf16[32,512,256]{2,1,0:T(8,128)(2,1)}), bf16[32,512,256]{2,1,0:T(8,128)(2,1)}, u32[]{:S(2)}, u32[]{:S(2)}) async-start(bf16[32,512,256]{2,1,0:T(8,128)(2,1)} %stack.8), calls=%async_computation | async-start | bytes 16777216 | tf_op jit(solution)/shard_map/all_to_all | solution.py:27
  29.3 65.2 %collective-permute-start.2 = (bf16[256,256]{1,0:T(8,128)(2,1)S(1)}, bf16[256,256]{1,0:T(8,128)(2,1)S(1)}, u32[]{:S(2)}, u32[]{:S(2)}) collective-permute-start(bf16[256,256]{1,0:T(8,128)(2,1)S(1)} %copy-done), channel_id=1, source_target_pairs={{0,1},{1,0},{2,3},{3,2},{4,5},{5,4},{6,7},{7,6},{8,9},{9,8},{10,11... | collective-permute-start | bytes 393224 | tf_op jit(solution)/shard_map/ppermute | solution.py:21
  146.1 16.8 %copy-start.1 = (f32[512]{0:T(512)S(1)}, f32[512]{0:T(512)}, u32[]{:S(2)}) copy-start(f32[512]{0:T(512)} %param.9) | copy-start | bytes 6148
  146.1 16.8 %copy-start.2 = (f32[256]{0:T(256)S(1)}, f32[256]{0:T(256)}, u32[]{:S(2)}) copy-start(f32[256]{0:T(256)} %param.10) | copy-start | bytes 3076
  146.1 102.7 %copy-start.3 = (f32[256]{0:T(256)S(1)}, f32[256]{0:T(256)}, u32[]{:S(2)}) copy-start(f32[256]{0:T(256)} %param.11) | copy-start | bytes 3076
  146.1 16.8 %collective-permute-start.3 = (f32[512,256]{0,1:T(8,128)S(1)}, f32[512,256]{0,1:T(8,128)S(1)}, u32[]{:S(2)}, u32[]{:S(2)}) collective-permute-start(f32[512,256]{0,1:T(8,128)S(1)} %fusion.2), channel_id=1, source_target_pairs={{0,1},{1,0},{2,3},{3,2},{4,5},{5,4},{6,7},{7,6},{8,9},{9,8},{10,11... | collective-permute-start | bytes 1572872 | tf_op jit(solution)/shard_map/ppermute | solution.py:44
